TPU v7x, 256 devices: a whole 4x4x8 slice. The times are simulated.
256 devices in a mesh: tile: 16 (over z, core), tensor: 16 (over y, x).
Axes of the slice: x: 4, y: 4, z: 8, core: 2. Of those that a mesh axis runs over, the one named last changes fastest.
Arguments:
- image_hidden: bfloat16 [8, 32, 32, 3072], P(None, 'tile', 'tensor'), may hold values from -6 to 6
- text_hidden: bfloat16 [8, 512, 3072], P(None, ('tile', 'tensor')), may hold values from -6 to 6
- latents: float32 [8, 32, 2048], P(None, 'tile', 'tensor'), may hold values from -6 to 6
- step_index: int32 [8], replicated, may hold values from 0 to 27
- anchor: int32 [8, 2], replicated, may hold values from 0 to 63
- text_len: int32 [8], replicated, may hold values from 64 to 512
- mod_image: float32 [8, 3, 3072], replicated, may hold values from -3 to 3
- mod_text: float32 [8, 3, 3072], replicated, may hold values from -3 to 3
- mod_mlp: float32 [8, 3, 3072], replicated, may hold values from -3 to 3
- mod_final: float32 [8, 2, 3072], replicated, may hold values from -3 to 3
- qkv_image: bfloat16 [3072, 3, 2048], P(None, None, 'tensor'), may hold values from -0.109375 to 0.109375
- qkv_text: bfloat16 [3072, 3, 2048], P(None, None, 'tensor'), may hold values from -0.109375 to 0.109375
- proj_image: bfloat16 [2048, 3072], P('tensor'), may hold values from -0.125 to 0.125
- proj_text: bfloat16 [2048, 3072], P('tensor'), may hold values from -0.125 to 0.125
- qk_gain: float32 [2, 2, 128], replicated, may hold values from 0.5 to 10
- mlp_expand: bfloat16 [3072, 6144], P(None, 'tensor'), may hold values from -0.109375 to 0.109375
- mlp_reduce: bfloat16 [6144, 3072], P('tensor'), may hold values from -0.078125 to 0.078125
- final_weight: bfloat16 [3072, 64], replicated, may hold values from -0.109375 to 0.109375
Outputs:
- image_out: bfloat16 [8, 32, 32, 3072], P(None, 'tile', 'tensor')
- text_out: bfloat16 [8, 512, 3072], P(None, ('tile', 'tensor'))
- latents_ext: float32 [8, 64, 2048], P(None, 'tile', 'tensor')
Inputs may be any that keep to these rules, and one draw needn't show every extreme that they name: text_len gives each request's live text tokens; slots at or past it take no part as keys. step_index is a step of the 28-step plan.
All inputs are finite; a program needn't handle non-finite values.
Results may differ from a plain program's by a relative error of at most 0.0085.
The roundings to bfloat16 on the way count: a program that leaves them out, or rounds other values in their place, can miss the bound.
Values may be sent and summed in bfloat16 or wider, within the bound.
No kernel may reach another device: no remote copies, remote signals or barrier semaphores. Data moves between devices by JAX's collectives and lax.ppermute only.
A program may use at most 128 MiB of HBM per device.

v0:
```python
import math
import jax
import jax.numpy as jnp
from jax import lax
from jax.sharding import PartitionSpec as P

HEAD_DIM = 128
GRID = 32
NSTEPS = 28
norm_eps = 1e-06
time_shift = 3.0


def padded(value, sides, width):
    for axis, dim in sides:
        size, length = (lax.axis_size(axis), value.shape[dim])
        up = [(i, (i + 1) % size) for i in range(size - 1)]
        down = [(j, i) for i, j in up]
        last = lax.slice_in_dim(value, length - width, length, axis=dim)
        leading = lax.slice_in_dim(value, 0, width, axis=dim)
        before = lax.ppermute(last, axis, up)
        after = lax.ppermute(leading, axis, down)
        value = jnp.concatenate([before, value, after], axis=dim)
    return value


def layer_norm(values):
    average = jnp.mean(values, -1, keepdims=True)
    centred = values - average
    spread = jnp.mean(centred * centred, -1, keepdims=True)
    return centred * lax.rsqrt(spread + norm_eps)


def modulate(hidden, shift, stretch):
    normed = layer_norm(hidden.astype(jnp.float32))
    return ((1.0 + stretch) * normed + shift).astype(jnp.bfloat16)


def rope_tables(row_ids, col_ids):
    pair_index = jnp.arange(64, dtype=jnp.int32)
    row_rank = (pair_index - 8).astype(jnp.float32)
    col_rank = (pair_index - 36).astype(jnp.float32)
    log_base = math.log(10000.0)
    row_freq = jnp.where(
        (pair_index >= 8) & (pair_index < 36), jnp.exp(-2.0 * row_rank / 56.0 * log_base), 0.0
    )
    col_freq = jnp.where(pair_index >= 36, jnp.exp(-2.0 * col_rank / 56.0 * log_base), 0.0)
    angles = row_ids[..., None] * row_freq + col_ids[..., None] * col_freq
    angles = jnp.repeat(angles, 2, axis=-1)
    sign_table = jnp.where(jnp.arange(128, dtype=jnp.int32) % 2 == 0, -1.0, 1.0).astype(jnp.float32)
    return (jnp.cos(angles), jnp.sin(angles) * sign_table)


def rotate(values, cos_table, sin_table):
    paired = values.reshape(values.shape[:-1] + (values.shape[-1] // 2, 2))
    swapped = jnp.flip(paired, -1).reshape(values.shape)
    return values * cos_table + swapped * sin_table


def head_norm(projected, head_gain):
    squares = jnp.mean(projected * projected, -1, keepdims=True)
    return projected * lax.rsqrt(squares + norm_eps) * head_gain


def sigma_of(step_float):
    level = 1.0 - step_float / NSTEPS
    return time_shift * level / (1.0 + (time_shift - 1.0) * level)


def key_usable(text_len, key_count, text_tile, block_len):
    key_pos = jnp.arange(key_count, dtype=jnp.int32)
    owner_tile = key_pos // block_len
    offset = key_pos % block_len
    text_pos = owner_tile * text_tile + offset
    return jnp.logical_or(offset[None, :] >= text_tile, text_pos[None, :] < text_len[:, None])


def per_device(
    image_hidden,
    text_hidden,
    latents,
    step_index,
    anchor,
    text_len,
    mod_image,
    mod_text,
    mod_mlp,
    mod_final,
    qkv_image,
    qkv_text,
    proj_image,
    proj_text,
    qk_gain,
    mlp_expand,
    mlp_reduce,
    final_weight,
):
    requests, tile_rows, tile_cols, model_width = image_hidden.shape
    local_cols = qkv_image.shape[2]
    local_heads = local_cols // HEAD_DIM
    local_units = mlp_expand.shape[1]
    image_all, text_all = (
        lax.all_gather(image_hidden, "tensor", axis=2, tiled=True),
        lax.all_gather(text_hidden, "tensor", axis=1, tiled=True),
    )
    image_mod = modulate(image_all, mod_image[:, 0, None, None, :], mod_image[:, 1, None, None, :])
    text_mod = modulate(text_all, mod_text[:, 0, None, :], mod_text[:, 1, None, :])
    text_tile = text_mod.shape[1]
    image_count = tile_rows * GRID
    block_len = text_tile + image_count
    tile_index = lax.axis_index("tile")
    token_index = jnp.arange(image_count, dtype=jnp.int32)
    row_ids = (anchor[:, 0:1] + tile_index * tile_rows + token_index[None, :] // GRID).astype(
        jnp.float32
    )
    col_ids = (anchor[:, 1:2] + token_index[None, :] % GRID).astype(jnp.float32)
    cos_table, sin_table = rope_tables(row_ids, col_ids)
    cos_table = cos_table[:, :, None, :]
    sin_table = sin_table[:, :, None, :]
    image_qkv = jnp.dot(
        image_mod.reshape(requests * image_count, model_width),
        qkv_image.reshape(model_width, 3 * local_cols),
        preferred_element_type=jnp.float32,
    ).reshape(requests, image_count, 3, local_heads, HEAD_DIM)
    text_qkv = jnp.dot(
        text_mod.reshape(requests * text_tile, model_width),
        qkv_text.reshape(model_width, 3 * local_cols),
        preferred_element_type=jnp.float32,
    ).reshape(requests, text_tile, 3, local_heads, HEAD_DIM)
    query = jnp.concatenate(
        [
            head_norm(text_qkv[:, :, 0], qk_gain[1, 0]).astype(jnp.bfloat16),
            rotate(head_norm(image_qkv[:, :, 0], qk_gain[0, 0]), cos_table, sin_table).astype(
                jnp.bfloat16
            ),
        ],
        1,
    )
    keys = jnp.concatenate(
        [
            head_norm(text_qkv[:, :, 1], qk_gain[1, 1]).astype(jnp.bfloat16),
            rotate(head_norm(image_qkv[:, :, 1], qk_gain[0, 1]), cos_table, sin_table).astype(
                jnp.bfloat16
            ),
        ],
        1,
    )
    values = jnp.concatenate([text_qkv[:, :, 2], image_qkv[:, :, 2]], 1).astype(jnp.bfloat16)
    score_scale = 1.0 / math.sqrt(HEAD_DIM)
    keys_all, values_all = (
        lax.all_gather(keys, "tile", axis=1, tiled=True),
        lax.all_gather(values, "tile", axis=1, tiled=True),
    )
    usable = key_usable(text_len, keys_all.shape[1], text_tile, block_len)[:, None, None, :]
    scores = (
        jnp.einsum("rqhd,rkhd->rhqk", query, keys_all, preferred_element_type=jnp.float32)
        * score_scale
    )
    row_top = jnp.max(jnp.where(usable, scores, -jnp.inf), -1, keepdims=True)
    weights_raw = jnp.where(usable, jnp.exp(scores - row_top), 0.0)
    weight_sum = jnp.sum(weights_raw, -1, keepdims=True)
    accum = jnp.einsum(
        "rhqk,rkhd->rhqd",
        weights_raw.astype(jnp.bfloat16),
        values_all,
        preferred_element_type=jnp.float32,
    )
    attended = (accum / weight_sum).transpose(0, 2, 1, 3).astype(jnp.bfloat16)
    text_term = jnp.dot(
        attended[:, :text_tile].reshape(requests * text_tile, local_cols),
        proj_text,
        preferred_element_type=jnp.float32,
    ).reshape(requests, text_tile, model_width)
    image_term = jnp.dot(
        attended[:, text_tile:].reshape(requests * image_count, local_cols),
        proj_image,
        preferred_element_type=jnp.float32,
    ).reshape(requests, tile_rows, GRID, model_width)
    image_gate = mod_image[:, 2, None, None, :]
    image_sum, text_sum = (
        lax.psum_scatter(image_term, "tensor", scatter_dimension=2, tiled=True),
        lax.psum_scatter(text_term, "tensor", scatter_dimension=1, tiled=True),
    )
    image_mid = (image_hidden.astype(jnp.float32) + image_gate * image_sum).astype(jnp.bfloat16)
    mlp_mod = modulate(image_mid, mod_mlp[:, 0, None, None, :], mod_mlp[:, 1, None, None, :])
    piece = lax.all_gather(mlp_mod, "tensor", axis=2, tiled=True)
    grown = jnp.dot(piece.reshape(-1, model_width), mlp_expand, preferred_element_type=jnp.float32)
    activated = (
        jax.nn.gelu(grown, approximate=True)
        .astype(jnp.bfloat16)
        .reshape(piece.shape[:-1] + (local_units,))
    )
    text_out = (text_hidden.astype(jnp.float32) + mod_text[:, 2, None, :] * text_sum).astype(
        jnp.bfloat16
    )
    mlp_term = jnp.dot(
        activated.reshape(requests * image_count, local_units),
        mlp_reduce,
        preferred_element_type=jnp.float32,
    ).reshape(requests, tile_rows, GRID, model_width)
    mlp_sum = lax.psum_scatter(mlp_term, "tensor", scatter_dimension=2, tiled=True)
    image_out = (image_mid.astype(jnp.float32) + mod_mlp[:, 2, None, None, :] * mlp_sum).astype(
        jnp.bfloat16
    )
    final_in = modulate(image_out, mod_final[:, 0, None, None, :], mod_final[:, 1, None, None, :])
    velocity = jnp.dot(
        final_in.reshape(requests * tile_rows * tile_cols, model_width),
        final_weight,
        preferred_element_type=jnp.float32,
    ).reshape(requests, tile_rows, tile_cols * final_weight.shape[1])
    step_float = step_index.astype(jnp.float32)
    time_delta = sigma_of(step_float + 1.0) - sigma_of(step_float)
    latents_next = latents + time_delta[:, None, None] * velocity
    latents_ext = padded(latents_next, (("tile", 1),), 1)
    return (image_out, text_out, latents_ext)


def solution(mesh):
    return jax.shard_map(
        per_device,
        mesh=mesh,
        in_specs=(
            P(None, "tile", "tensor", None),
            P(None, ("tile", "tensor"), None),
            P(None, "tile", "tensor"),
            P(),
            P(),
            P(),
            P(),
            P(),
            P(),
            P(),
            P(None, None, "tensor"),
            P(None, None, "tensor"),
            P("tensor", None),
            P("tensor", None),
            P(),
            P(None, "tensor"),
            P("tensor", None),
            P(),
        ),
        out_specs=(
            P(None, "tile", "tensor", None),
            P(None, ("tile", "tensor"), None),
            P(None, "tile", "tensor"),
        ),
        check_vma=False,
    )
```

profile of v0, /device:TPU:32, one launch (start us, length us, event | category | flops | bytes accessed | tf_op | source)
XLA Modules:
  0.0 585.7 jit_solution(4433946694455913558)
XLA Ops:
  7.2 1.7 copy.62
  9.0 1.7 copy.61
  10.8 4.3 copy.66
  15.5 1.0 fusion.99
  16.6 0.9 copy.68
  17.5 0.9 copy.70
  18.5 4.3 copy.63
  23.9 1.7 slice_bitcast_fusion.3
  25.6 36.5 %all-gather.6.cloned.1.call-done = bf16[8,32,3072]{2,0,1:T(8,128)(2,1)} async-done(((bf16[8,2,3072]{2,0,1:T(8,128)(2,1)}), bf16[8,32,3072]{2,0,1:T(8,128)(2,1)}) %all-gather.6.cloned.1.call-update) | async-done | bytes 1572880 | tf_op jit(solution)/shard_map/all_gather | solution.py:104
  62.1 1.8 convert_reduce_fusion.1
  63.9 2.0 fusion.13
  65.9 2.8 fusion.38
  70.8 46.7 %all-gather.8.cloned.1.call-done = bf16[8,2,32,3072]{3,0,1,2:T(8,128)(2,1)} async-done(((bf16[8,2,2,3072]{3,0,1,2:T(8,128)(2,1)}), bf16[8,2,32,3072]{3,0,1,2:T(8,128)(2,1)}) %all-gather.8.cloned.1.call-update) | async-done | bytes 3145744 | tf_op jit(solution)/shard_map/all_gather | solution.py:103
  117.5 5.4 convert_reduce_fusion
  122.9 3.2 fusion.3
  126.1 7.0 %fusion.6 = bf16[8,2,32,3072]{3,2,1,0:T(8,128)(2,1)S(1)} fusion(f32[8,3072]{1,0:T(8,128)S(1)} %get-tuple-element.32, f32[8,2,32]{2,1,0:T(2,128)S(1)} %add_rsqrt_fusion.3, f32[8,2,32]{2,1,0:T(2,128)S(1)} %broadcast_multiply_fusion.1, f32[8,3072]{1,0:T(8,128)S(1)} %get-tuple-element.33, bf16[8,2,32,3072]{3,0,1,2:T(8,128)(2,1)S(1)} %copy-done.1), kind=kLoop, calls=%fused_computation.8 | loop fusion | flops 9437184 | bytes 6492160 | tf_op jit(solution)/shard_map/convert_element_type | solution.py:36
  133.1 1.8 fusion.35
  135.9 2.0 copy.74
  137.9 2.0 multiply_multiply_fusion.1
  139.9 1.9 rev.8
  141.8 1.9 copy.75
  143.7 1.0 copy.69
  144.7 2.0 multiply_multiply_fusion.2
  146.7 1.9 rev.7
  148.6 1.2 copy.71
  149.8 1.3 fusion.93
  151.2 1.5 pad_maximum_fusion
  152.8 0.9 fusion.106
  156.1 36.4 %all-gather.10.cloned.1.call-done = bf16[8,1536,1,128]{3,1,0,2:T(8,128)(2,1)} async-done(((bf16[8,96,1,128]{3,1,0,2:T(8,128)(2,1)}), bf16[8,1536,1,128]{3,1,0,2:T(8,128)(2,1)}) %all-gather.10.cloned.1.call-update) | async-done | bytes 3145744 | tf_op jit(solution)/shard_map/all_gather | solution.py:151
  192.5 3.0 fusion.19
  195.6 3.0 fusion.132
  198.5 36.0 %all-gather.12.cloned.1.call-done = bf16[8,1536,1,128]{3,1,0,2:T(8,128)(2,1)} async-done(((bf16[8,96,1,128]{3,1,0,2:T(8,128)(2,1)}), bf16[8,1536,1,128]{3,1,0,2:T(8,128)(2,1)}) %all-gather.12.cloned.1.call-update) | async-done | bytes 3145744 | tf_op jit(solution)/shard_map/all_gather | solution.py:152
  234.5 3.5 fusion.53
  238.7 3.6 fusion.68
  243.3 84.6 %reduce-scatter.4.cloned.1.call-done = f32[8,2,2,3072]{3,0,1,2:T(8,128)} async-done(((f32[8,2,32,3072]{3,0,1,2:T(8,128)}), f32[8,2,2,3072]{3,0,1,2:T(8,128)}) %reduce-scatter.4.cloned.1.call-update) | async-done | bytes 393232 | tf_op jit(solution)/shard_map/reduce_scatter | solution.py:181
  327.9 1.2 convert_reduce_fusion.2
  330.5 52.7 %all-gather.14.cloned.1.call-done = bf16[8,2,32,3072]{3,0,1,2:T(8,128)(2,1)} async-done(((bf16[8,2,2,3072]{3,0,1,2:T(8,128)(2,1)}), bf16[8,2,32,3072]{3,0,1,2:T(8,128)(2,1)}) %all-gather.14.cloned.1.call-update) | async-done | bytes 3145744 | tf_op jit(solution)/shard_map/all_gather | solution.py:186
  383.2 5.3 copy.79
  388.4 8.8 %fusion.83 = f32[512,3072]{1,0:T(8,128)} fusion(bf16[384,3072]{1,0:T(8,128)(2,1)S(1)} %copy-done, bf16[512,3072]{1,0:T(8,128)(2,1)} %bitcast.160, bf16[3072,384]{1,0:T(8,128)(2,1)} %param.33), kind=kOutput, calls=%fused_computation.76 | convolution fusion | flops 2417688576 | bytes 14155776 | tf_op jit(solution)/shard_map/dot_general | solution.py:196
  397.2 9.1 %copy.80 = f32[8,2,32,3072]{3,0,1,2:T(8,128)} copy(f32[8,2,32,3072]{3,2,1,0:T(8,128)} %bitcast.158) | data formatting | bytes 12582912 | tf_op jit(solution)/shard_map/reshape | solution.py:200
  406.4 0.9 slice_bitcast_fusion.9
  407.5 2.3 fusion.66
  410.9 80.8 %reduce-scatter.6.cloned.1.call-done = f32[8,2,2,3072]{3,0,1,2:T(8,128)} async-done(((f32[8,2,32,3072]{3,0,1,2:T(8,128)}), f32[8,2,2,3072]{3,0,1,2:T(8,128)}) %reduce-scatter.6.cloned.1.call-update) | async-done | bytes 393232 | tf_op jit(solution)/shard_map/reduce_scatter | solution.py:201
  491.7 1.1 convert_reduce_fusion.3
  494.0 1.9 collective-permute-start
  495.9 3.6 collective-permute-start.1
  499.5 76.0 %reduce-scatter.8.cloned.1.call-done = f32[8,2,3072]{2,0,1:T(8,128)} async-done(((f32[8,32,3072]{2,0,1:T(8,128)}), f32[8,2,3072]{2,0,1:T(8,128)}) %reduce-scatter.8.cloned.1.call-update) | async-done | bytes 196624 | tf_op jit(solution)/shard_map/reduce_scatter | solution.py:182
  575.6 1.0 add_convert_fusion.1
  (108 shorter events, 15.0 us)
Async XLA Ops:
  7.2 381.3 %copy-start = (bf16[384,3072]{1,0:T(8,128)(2,1)S(1)}, bf16[384,3072]{1,0:T(8,128)(2,1)}, u32[]{:S(2)}) copy-start(bf16[384,3072]{1,0:T(8,128)(2,1)} %param.34) | copy-start | bytes 7077892
  7.2 7.9 %copy-start.16 = (f32[2,2,128]{2,1,0:T(2,128)S(1)}, f32[2,2,128]{2,1,0:T(2,128)}, u32[]{:S(2)}) copy-start(f32[2,2,128]{2,1,0:T(2,128)} %param.32) | copy-start | bytes 6148
  7.2 8.2 %copy-start.17 = (s32[8,2]{0,1:T(2,128)S(1)}, s32[8,2]{0,1:T(2,128)}, u32[]{:S(2)}) copy-start(s32[8,2]{0,1:T(2,128)} %param.22) | copy-start | bytes 196
  7.2 54.9 %all-gather.6.cloned.1.call-start = ((), (), s32[]{:S(2)}) async-start(), calls=%async_computation.3 | async-start | bytes 1671168 | tf_op jit(solution)/shard_map/all_gather | solution.py:104
  9.0 108.5 %all-gather.8.cloned.1.call-start = ((), (), s32[]{:S(2)}) async-start(), calls=%async_computation.4 | async-start | bytes 3342336 | tf_op jit(solution)/shard_map/all_gather | solution.py:103
  10.7 181.8 %all-gather.10.cloned.1.call-start = ((), (), s32[]{:S(2)}) async-start(), calls=%async_computation.5 | async-start | bytes 3342336 | tf_op jit(solution)/shard_map/all_gather | solution.py:151
  17.5 5.7 copy-start.11
  62.1 3.8 copy-start.2
  68.7 0.8 copy-start.4
  117.5 5.4 copy-start.1
  126.0 7.1 %copy-start.3 = (bf16[3072,3,128]{0,2,1:T(8,128)(2,1)S(1)}, bf16[3072,3,128]{0,2,1:T(8,128)(2,1)}, u32[]{:S(2)}) copy-start(bf16[3072,3,128]{0,2,1:T(8,128)(2,1)} %copy.66) | copy-start | bytes 7077892
  152.7 81.8 %all-gather.12.cloned.1.call-start = ((), (), s32[]{:S(2)}) async-start(), calls=%async_computation.6 | async-start | bytes 3342336 | tf_op jit(solution)/shard_map/all_gather | solution.py:152
  154.4 173.5 %reduce-scatter.4.cloned.1.call-start = ((), (), s32[]{:S(2)}) async-start(), calls=%async_computation.7 | async-start | bytes 6684672 | tf_op jit(solution)/shard_map/reduce_scatter | solution.py:181
  234.5 4.2 copy-start.5
  238.0 0.7 copy-start.14
  242.3 1.0 copy-start.12
  242.3 85.6 %copy-start.6 = (bf16[8,2,2,3072]{3,2,1,0:T(2,128)(2,1)S(1)}, bf16[8,2,2,3072]{3,2,1,0:T(2,128)(2,1)}, u32[]{:S(2)}) copy-start(bf16[8,2,2,3072]{3,2,1,0:T(2,128)(2,1)} %param.18) | copy-start | bytes 589828
  242.3 85.6 %copy-start.8 = (f32[8,3072]{1,0:T(8,128)S(1)}, f32[8,3072]{1,0:T(8,128)}, u32[]{:S(2)}) copy-start(f32[8,3072]{1,0:T(8,128)} %get-tuple-element.31) | copy-start | bytes 294916
  242.4 140.8 %all-gather.14.cloned.1.call-start = ((), (), s32[]{:S(2)}) async-start(), calls=%async_computation.8 | async-start | bytes 3342336 | tf_op jit(solution)/shard_map/all_gather | solution.py:186
  330.2 161.5 %reduce-scatter.6.cloned.1.call-start = ((), (), s32[]{:S(2)}) async-start(), calls=%async_computation.9 | async-start | bytes 6684672 | tf_op jit(solution)/shard_map/reduce_scatter | solution.py:201
  406.3 1.2 copy-start.7
  406.3 169.2 %reduce-scatter.8.cloned.1.call-start = ((), (), s32[]{:S(2)}) async-start(), calls=%async_computation.10 | async-start | bytes 3342336 | tf_op jit(solution)/shard_map/reduce_scatter | solution.py:182
  407.5 2.3 copy-start.18
  409.7 0.9 copy-start.13
  409.7 83.8 %copy-start.9 = (bf16[3072,64]{0,1:T(8,128)(2,1)S(1)}, bf16[3072,64]{0,1:T(8,128)(2,1)}, u32[]{:S(2)}) copy-start(bf16[3072,64]{0,1:T(8,128)(2,1)} %param.35) | copy-start | bytes 1179652
  409.8 84.1 %copy-start.15 = (f32[8,2,128]{2,1,0:T(2,128)S(1)}, f32[8,2,128]{2,1,0:T(2,128)}, u32[]{:S(2)}) copy-start(f32[8,2,128]{2,1,0:T(2,128)} %param.20) | copy-start | bytes 24580
  409.8 165.8 %copy-start.10 = (f32[8,3072]{1,0:T(8,128)S(1)}, f32[8,3072]{1,0:T(8,128)}, u32[]{:S(2)}) copy-start(f32[8,3072]{1,0:T(8,128)} %get-tuple-element.25) | copy-start | bytes 294916
  494.0 84.2 %collective-permute-start = (f32[8,1,128]{2,1,0:T(1,128)S(1)}, f32[8,1,128]{2,1,0:T(1,128)S(1)}, u32[]{:S(2)}, u32[]{:S(2)}) collective-permute-start(f32[8,1,128]{2,1,0:T(1,128)S(1)} %get-tuple-element.38), channel_id=1, source_target_pairs={{0,16},{16,32},{32,48},{48,64},{64,80},{80,96},{96,112},{112,128},... | collective-permute-start | bytes 12296 | tf_op jit(solution)/shard_map/ppermute | solution.py:21
  495.9 82.3 %collective-permute-start.1 = (f32[8,1,128]{2,1,0:T(1,128)S(1)}, f32[8,1,128]{2,1,0:T(1,128)S(1)}, u32[]{:S(2)}, u32[]{:S(2)}) collective-permute-start(f32[8,1,128]{2,1,0:T(1,128)S(1)} %get-tuple-element.39), channel_id=1, source_target_pairs={{16,0},{32,16},{48,32},{64,48},{80,64},{96,80},{112,96},{128,112},... | collective-permute-start | bytes 12296 | tf_op jit(solution)/shard_map/ppermute | solution.py:22
Sparse Core Ops, SparseCore 0:
  10.5 51.5 all-gather.5
  65.1 52.3 all-gather.7
  152.8 39.6 all-gather.9
  194.8 39.6 all-gather.11
  242.5 85.3 reduce-scatter.3
  330.8 52.3 all-gather.13
  406.5 85.2 reduce-scatter.5
  495.3 80.1 reduce-scatter.7
where the time goes:
time: 587 us; the launch traced here: 586 us
  waiting for transfers between devices  450 us (77%)
  local copies, waits for them, and re-layouts  47.8 us (8%)
  other arithmetic  41.3 us (7%)
  matrix products  26 us (4%)
  between operations  14.5 us (2%)
  starting transfers between devices  6.11 us (1%)
    reduce_scatter x1, waiting for transfers between devices, per_device(): lax.psum_scatter(image_term, 'tensor', scatter_dimension=2, tiled=True)  84.6 us
    reduce_scatter x1, waiting for transfers between devices, per_device(): lax.psum_scatter(mlp_term, 'tensor', scatter_dimension=2, tiled=True)  80.8 us
    reduce_scatter x1, waiting for transfers between devices, per_device(): lax.psum_scatter(text_term, 'tensor', scatter_dimension=1, tiled=True)  76 us
    all_gather x1, waiting for transfers between devices, per_device(): piece = lax.all_gather(mlp_mod, 'tensor', axis=2, tiled=True)  52.7 us
    all_gather x1, waiting for transfers between devices, per_device(): lax.all_gather(image_hidden, 'tensor', axis=2, tiled=True)  46.7 us
    all_gather x1, waiting for transfers between devices, per_device(): lax.all_gather(text_hidden, 'tensor', axis=1, tiled=True)  36.5 us
    all_gather x1, waiting for transfers between devices, per_device(): lax.all_gather(keys, 'tile', axis=1, tiled=True)  36.4 us
    all_gather x1, waiting for transfers between devices, per_device(): lax.all_gather(values, 'tile', axis=1, tiled=True)  36 us
  transfers between devices with their start and end apart: 10, of which 8 were waited for; matrix products, arithmetic and copies ran while one was open for 7% of the time, Pallas kernels for 0%

commit v1 on v0

--- a/solution.py
+++ b/solution.py
@@ -9,6 +9,19 @@
 NSTEPS = 28
 norm_eps = 1e-06
 time_shift = 3.0
+
+
+def gather_around(value, axis, dim):
+    ways = lax.axis_size(axis)
+    up = [(d, (d + 1) % ways) for d in range(ways)]
+    down = [(d, (d - 1) % ways) for d in range(ways)]
+    earlier, later = ([value], [value])
+    for _ in range(ways // 2):
+        earlier.append(lax.ppermute(earlier[-1], axis, up))
+    for _ in range((ways - 1) // 2):
+        later.append(lax.ppermute(later[-1], axis, down))
+    line = jnp.concatenate([*earlier[::-1], *later[1:]], axis=dim)
+    return jnp.roll(line, (lax.axis_index(axis) - ways // 2) * value.shape[dim], axis=dim)
 
 
 def padded(value, sides, width):
@@ -101,7 +114,7 @@
     local_units = mlp_expand.shape[1]
     image_all, text_all = (
         lax.all_gather(image_hidden, "tensor", axis=2, tiled=True),
-        lax.all_gather(text_hidden, "tensor", axis=1, tiled=True),
+        gather_around(text_hidden, "tensor", 1),
     )
     image_mod = modulate(image_all, mod_image[:, 0, None, None, :], mod_image[:, 1, None, None, :])
     text_mod = modulate(text_all, mod_text[:, 0, None, :], mod_text[:, 1, None, :])

time: 587 us -> 594 us (1.012); the launches traced: 586 us -> 583 us
  waiting for transfers between devices: 450 us -> 383 us
  starting transfers between devices: 6.11 us -> 44.1 us
  local copies, waits for them, and re-layouts: 47.8 us -> 67.8 us
    all_gather x1, waiting for transfers between devices: 46.7 us -> 0.01 us  [per_device(): lax.all_gather(image_hidden, 'tensor', axis=2, tiled=True)]
    ppermute x0 -> x15, starting transfers between devices: none -> 38 us  [the longest x7 36.2 us: gather_around(): later.append(lax.ppermute(later[-1], axis, down))]
    all_gather x1 -> x0, waiting for transfers between devices: 36.5 us -> none  [per_device(): lax.all_gather(text_hidden, 'tensor', axis=1, tiled=True)]
    concatenate x0 -> x1, local copies, waits for them, and re-layouts: none -> 21.5 us  [gather_around(): jnp.roll(line, (lax.axis_index(axis) - ways // 2) * value.shape[dim], axi...]
    ppermute x0 -> x15, waiting for transfers between devices: none -> 17.8 us  [the longest x8 15.8 us: gather_around(): earlier.append(lax.ppermute(earlier[-1], axis, up))]
    unnamed x45 -> x72, local copies, waits for them, and re-layouts: 17.6 us -> 15.3 us
  transfers between devices with their start and end apart: 10 -> 24, of which waited for: 8 -> 12; matrix products, arithmetic and copies ran while one was open for 7% -> 12% of each run, Pallas kernels for 0% -> 0%
where the time goes in v1:
time: 594 us; the launch traced here: 583 us
  waiting for transfers between devices  383 us (64%)
  local copies, waits for them, and re-layouts  67.8 us (11%)
  other arithmetic  46.6 us (8%)
  starting transfers between devices  44.1 us (7%)
  matrix products  26.2 us (4%)
  between operations  15.1 us (3%)
    reduce_scatter x1, waiting for transfers between devices, per_device(): lax.psum_scatter(image_term, 'tensor', scatter_dimension=2, tiled=True)  84 us
    reduce_scatter x1, waiting for transfers between devices, per_device(): lax.psum_scatter(mlp_term, 'tensor', scatter_dimension=2, tiled=True)  80.2 us
    reduce_scatter x1, waiting for transfers between devices, per_device(): lax.psum_scatter(text_term, 'tensor', scatter_dimension=1, tiled=True)  75.1 us
    all_gather x1, waiting for transfers between devices, per_device(): piece = lax.all_gather(mlp_mod, 'tensor', axis=2, tiled=True)  52.7 us
    all_gather x1, waiting for transfers between devices, per_device(): lax.all_gather(keys, 'tile', axis=1, tiled=True)  37.2 us
    ppermute x7, starting transfers between devices, gather_around(): later.append(lax.ppermute(later[-1], axis, down))  36.2 us
    all_gather x1, waiting for transfers between devices, per_device(): lax.all_gather(values, 'tile', axis=1, tiled=True)  36 us
    concatenate x1, local copies, waits for them, and re-layouts, gather_around(): jnp.roll(line, (lax.axis_index(axis) - ways // 2) * value.shape[dim], axi...  21.5 us
  transfers between devices with their start and end apart: 24, of which 12 were waited for; matrix products, arithmetic and copies ran while one was open for 12% of the time, Pallas kernels for 0%

profile of v1, /device:TPU:32, one launch (start us, length us, event | category | flops | bytes accessed | tf_op | source)
XLA Modules:
  0.0 583.1 jit_solution(13688114268853289919)
XLA Ops:
  7.2 1.8 copy.57
  10.7 3.9 collective-permute-start.8
  14.5 1.7 slice_bitcast_fusion.3
  18.8 5.4 collective-permute-start.9
  24.2 2.5 collective-permute-done.1
  26.8 5.4 collective-permute-start.10
  32.2 2.8 collective-permute-done.2
  35.0 5.4 collective-permute-start.11
  40.4 2.5 collective-permute-done.3
  42.9 5.4 collective-permute-start.12
  48.4 2.5 collective-permute-done.4
  51.9 4.3 copy.58
  56.2 4.4 copy.61
  60.6 5.4 collective-permute-start.13
  69.6 5.3 collective-permute-start.14
  75.5 1.9 collective-permute-done.14
  77.5 5.6 collective-permute-done.7
  83.1 21.5 %concatenate.31 = bf16[8,64,3072]{2,1,0:T(8,128)(2,1)} concatenate(bf16[8,2,3072]{2,1,0:T(2,128)(2,1)S(1)} %collective-permute-done.7, bf16[8,2,3072]{2,1,0:T(2,128)(2,1)} %collective-permute-done.6, bf16[8,2,3072]{2,1,0:T(2,128)(2,1)} %collective-permute-done.5, bf16[8,2,3072]{2,1,0:T(2,128)(2,1)} %copy-done.22, bf16[8,2,3072]{2,1,0:T(2,128)(2,1)} %copy-done.20, ...), dimensions={1} | concatenate | bytes 6291456 | tf_op jit(solution)/shard_map/jit(_roll_dynamic)/concatenate | solution.py:24
  104.6 2.3 convert_reduce_fusion.1
  106.9 2.5 fusion.13
  109.4 2.9 fusion.38
  113.9 5.4 convert_reduce_fusion
  119.3 3.2 fusion.3
  122.5 7.1 %fusion.6 = bf16[8,2,32,3072]{3,2,1,0:T(8,128)(2,1)S(1)} fusion(f32[8,3072]{1,0:T(8,128)S(1)} %copy-done.12, f32[8,2,32]{2,1,0:T(2,128)S(1)} %add_rsqrt_fusion, f32[8,2,32]{2,1,0:T(2,128)S(1)} %broadcast_multiply_fusion, f32[8,3072]{1,0:T(8,128)S(1)} %copy-done.13, bf16[8,2,32,3072]{3,0,1,2:T(8,128)(2,1)S(1)} %copy-done.1), kind=kLoop, calls=%fused_computation.8 | loop fusion | flops 9437184 | bytes 6492160 | tf_op jit(solution)/shard_map/convert_element_type | solution.py:49
  129.6 1.8 fusion.35
  132.4 1.9 copy.68
  134.3 2.1 multiply_multiply_fusion.1
  136.4 1.9 rev.8
  138.3 1.9 copy.69
  141.2 2.0 multiply_multiply_fusion.2
  143.2 1.9 rev.7
  146.4 2.0 fusion.94
  151.8 37.2 %all-gather.7.cloned.1.call-done = bf16[8,1536,1,128]{3,1,0,2:T(8,128)(2,1)} async-done(((bf16[8,96,1,128]{3,1,0,2:T(8,128)(2,1)}), bf16[8,1536,1,128]{3,1,0,2:T(8,128)(2,1)}) %all-gather.7.cloned.1.call-update) | async-done | bytes 3145744 | tf_op jit(solution)/shard_map/all_gather | solution.py:164
  189.0 3.1 fusion.19
  192.2 3.0 fusion.134
  195.1 36.0 %all-gather.9.cloned.1.call-done = bf16[8,1536,1,128]{3,1,0,2:T(8,128)(2,1)} async-done(((bf16[8,96,1,128]{3,1,0,2:T(8,128)(2,1)}), bf16[8,1536,1,128]{3,1,0,2:T(8,128)(2,1)}) %all-gather.9.cloned.1.call-update) | async-done | bytes 3145744 | tf_op jit(solution)/shard_map/all_gather | solution.py:165
  231.1 3.5 fusion.54
  235.3 3.6 fusion.69
  240.5 84.0 %reduce-scatter.4.cloned.1.call-done = f32[8,2,2,3072]{3,0,1,2:T(8,128)} async-done(((f32[8,2,32,3072]{3,0,1,2:T(8,128)}), f32[8,2,2,3072]{3,0,1,2:T(8,128)}) %reduce-scatter.4.cloned.1.call-update) | async-done | bytes 393232 | tf_op jit(solution)/shard_map/reduce_scatter | solution.py:194
  327.1 52.7 %all-gather.11.cloned.1.call-done = bf16[8,2,32,3072]{3,0,1,2:T(8,128)(2,1)} async-done(((bf16[8,2,2,3072]{3,0,1,2:T(8,128)(2,1)}), bf16[8,2,32,3072]{3,0,1,2:T(8,128)(2,1)}) %all-gather.11.cloned.1.call-update) | async-done | bytes 3145744 | tf_op jit(solution)/shard_map/all_gather | solution.py:199
  379.8 5.2 copy.71
  385.1 8.8 %fusion.84 = f32[512,3072]{1,0:T(8,128)} fusion(bf16[384,3072]{1,0:T(8,128)(2,1)S(1)} %copy-done, bf16[512,3072]{1,0:T(8,128)(2,1)} %bitcast.160, bf16[3072,384]{1,0:T(8,128)(2,1)} %param.33), kind=kOutput, calls=%fused_computation.77 | convolution fusion | flops 2417688576 | bytes 14155776 | tf_op jit(solution)/shard_map/dot_general | solution.py:209
  393.8 9.1 %copy.72 = f32[8,2,32,3072]{3,0,1,2:T(8,128)} copy(f32[8,2,32,3072]{3,2,1,0:T(8,128)} %bitcast.158) | data formatting | bytes 12582912 | tf_op jit(solution)/shard_map/reshape | solution.py:213
  404.1 2.3 fusion.67
  408.4 80.2 %reduce-scatter.6.cloned.1.call-done = f32[8,2,2,3072]{3,0,1,2:T(8,128)} async-done(((f32[8,2,32,3072]{3,0,1,2:T(8,128)}), f32[8,2,2,3072]{3,0,1,2:T(8,128)}) %reduce-scatter.6.cloned.1.call-update) | async-done | bytes 393232 | tf_op jit(solution)/shard_map/reduce_scatter | solution.py:214
  491.8 1.9 collective-permute-start.15
  493.7 3.6 collective-permute-start.16
  497.4 75.1 %reduce-scatter.8.cloned.1.call-done = f32[8,2,3072]{2,0,1:T(8,128)} async-done(((f32[8,32,3072]{2,0,1:T(8,128)}), f32[8,2,3072]{2,0,1:T(8,128)}) %reduce-scatter.8.cloned.1.call-update) | async-done | bytes 196624 | tf_op jit(solution)/shard_map/reduce_scatter | solution.py:195
  (160 shorter events, 32.1 us)
Async XLA Ops:
  7.2 377.9 %copy-start = (bf16[384,3072]{1,0:T(8,128)(2,1)S(1)}, bf16[384,3072]{1,0:T(8,128)(2,1)}, u32[]{:S(2)}) copy-start(bf16[384,3072]{1,0:T(8,128)(2,1)} %param.34) | copy-start | bytes 7077892
  7.2 106.7 %all-gather.5.cloned.1.call-start = ((), (), s32[]{:S(2)}) async-start(), calls=%async_computation.3 | async-start | bytes 3342336 | tf_op jit(solution)/shard_map/all_gather | solution.py:116
  9.1 180.0 %all-gather.7.cloned.1.call-start = ((), (), s32[]{:S(2)}) async-start(), calls=%async_computation.4 | async-start | bytes 3342336 | tf_op jit(solution)/shard_map/all_gather | solution.py:164
  9.1 9.6 %collective-permute-start = (bf16[8,2,3072]{2,1,0:T(2,128)(2,1)}, bf16[8,2,3072]{2,1,0:T(2,128)(2,1)S(1)}, u32[]{:S(2)}, u32[]{:S(2)}) collective-permute-start(bf16[8,2,3072]{2,1,0:T(2,128)(2,1)} %param.19), channel_id=1, source_target_pairs={{0,1},{1,2},{2,3},{3,4},{4,5},{5,6},{6,7},{7,8},{8,9},{9,10},{10,1... | collective-permute-start | bytes 294920 | tf_op jit(solution)/shard_map/ppermute | solution.py:20
  10.7 8.1 %collective-permute-start.8 = (bf16[8,2,3072]{2,1,0:T(2,128)(2,1)}, bf16[8,2,3072]{2,1,0:T(2,128)(2,1)S(1)}, u32[]{:S(2)}, u32[]{:S(2)}) collective-permute-start(bf16[8,2,3072]{2,1,0:T(2,128)(2,1)} %param.19), channel_id=1, source_target_pairs={{0,15},{1,0},{2,1},{3,2},{4,3},{5,4},{6,5},{7,6},{8,7},{9,8},{10,9... | collective-permute-start | bytes 294920 | tf_op jit(solution)/shard_map/ppermute | solution.py:22
  18.7 41.9 %copy-start.14 = (bf16[8,2,3072]{2,1,0:T(2,128)(2,1)}, bf16[8,2,3072]{2,1,0:T(2,128)(2,1)S(1)}, u32[]{:S(2)}) copy-start(bf16[8,2,3072]{2,1,0:T(2,128)(2,1)S(1)} %collective-permute-done) | copy-start | bytes 294916
  18.7 8.0 %collective-permute-start.1 = (bf16[8,2,3072]{2,1,0:T(2,128)(2,1)S(1)}, bf16[8,2,3072]{2,1,0:T(2,128)(2,1)S(1)}, u32[]{:S(2)}, u32[]{:S(2)}) collective-permute-start(bf16[8,2,3072]{2,1,0:T(2,128)(2,1)S(1)} %collective-permute-done), channel_id=1, source_target_pairs={{0,1},{1,2},{2,3},{3,4},{4,5},{5,6},{6,7},{7,8},{8,9},{9,10},{10,1... | collective-permute-start | bytes 294920 | tf_op jit(solution)/shard_map/ppermute | solution.py:20
  18.8 41.8 %copy-start.15 = (bf16[8,2,3072]{2,1,0:T(2,128)(2,1)}, bf16[8,2,3072]{2,1,0:T(2,128)(2,1)S(1)}, u32[]{:S(2)}) copy-start(bf16[8,2,3072]{2,1,0:T(2,128)(2,1)S(1)} %collective-permute-done.8) | copy-start | bytes 294916
  18.8 7.9 %collective-permute-start.9 = (bf16[8,2,3072]{2,1,0:T(2,128)(2,1)S(1)}, bf16[8,2,3072]{2,1,0:T(2,128)(2,1)S(1)}, u32[]{:S(2)}, u32[]{:S(2)}) collective-permute-start(bf16[8,2,3072]{2,1,0:T(2,128)(2,1)S(1)} %collective-permute-done.8), channel_id=1, source_target_pairs={{0,15},{1,0},{2,1},{3,2},{4,3},{5,4},{6,5},{7,6},{8,7},{9,8},{10,9... | collective-permute-start | bytes 294920 | tf_op jit(solution)/shard_map/ppermute | solution.py:22
  26.7 24.1 %copy-start.16 = (bf16[8,2,3072]{2,1,0:T(2,128)(2,1)}, bf16[8,2,3072]{2,1,0:T(2,128)(2,1)S(1)}, u32[]{:S(2)}) copy-start(bf16[8,2,3072]{2,1,0:T(2,128)(2,1)S(1)} %collective-permute-done.1) | copy-start | bytes 294916
  26.7 8.2 %collective-permute-start.2 = (bf16[8,2,3072]{2,1,0:T(2,128)(2,1)S(1)}, bf16[8,2,3072]{2,1,0:T(2,128)(2,1)S(1)}, u32[]{:S(2)}, u32[]{:S(2)}) collective-permute-start(bf16[8,2,3072]{2,1,0:T(2,128)(2,1)S(1)} %collective-permute-done.1), channel_id=1, source_target_pairs={{0,1},{1,2},{2,3},{3,4},{4,5},{5,6},{6,7},{7,8},{8,9},{9,10},{10,1... | collective-permute-start | bytes 294920 | tf_op jit(solution)/shard_map/ppermute | solution.py:20
  26.7 24.1 %copy-start.17 = (bf16[8,2,3072]{2,1,0:T(2,128)(2,1)}, bf16[8,2,3072]{2,1,0:T(2,128)(2,1)S(1)}, u32[]{:S(2)}) copy-start(bf16[8,2,3072]{2,1,0:T(2,128)(2,1)S(1)} %collective-permute-done.9) | copy-start | bytes 294916
  26.8 8.3 %collective-permute-start.10 = (bf16[8,2,3072]{2,1,0:T(2,128)(2,1)S(1)}, bf16[8,2,3072]{2,1,0:T(2,128)(2,1)S(1)}, u32[]{:S(2)}, u32[]{:S(2)}) collective-permute-start(bf16[8,2,3072]{2,1,0:T(2,128)(2,1)S(1)} %collective-permute-done.9), channel_id=1, source_target_pairs={{0,15},{1,0},{2,1},{3,2},{4,3},{5,4},{6,5},{7,6},{8,7},{9,8},{10,9... | collective-permute-start | bytes 294920 | tf_op jit(solution)/shard_map/ppermute | solution.py:22
  34.9 15.9 %copy-start.18 = (bf16[8,2,3072]{2,1,0:T(2,128)(2,1)}, bf16[8,2,3072]{2,1,0:T(2,128)(2,1)S(1)}, u32[]{:S(2)}) copy-start(bf16[8,2,3072]{2,1,0:T(2,128)(2,1)S(1)} %collective-permute-done.2) | copy-start | bytes 294916
  34.9 7.9 %collective-permute-start.3 = (bf16[8,2,3072]{2,1,0:T(2,128)(2,1)S(1)}, bf16[8,2,3072]{2,1,0:T(2,128)(2,1)S(1)}, u32[]{:S(2)}, u32[]{:S(2)}) collective-permute-start(bf16[8,2,3072]{2,1,0:T(2,128)(2,1)S(1)} %collective-permute-done.2), channel_id=1, source_target_pairs={{0,1},{1,2},{2,3},{3,4},{4,5},{5,6},{6,7},{7,8},{8,9},{9,10},{10,1... | collective-permute-start | bytes 294920 | tf_op jit(solution)/shard_map/ppermute | solution.py:20
  35.0 15.8 %copy-start.19 = (bf16[8,2,3072]{2,1,0:T(2,128)(2,1)}, bf16[8,2,3072]{2,1,0:T(2,128)(2,1)S(1)}, u32[]{:S(2)}) copy-start(bf16[8,2,3072]{2,1,0:T(2,128)(2,1)S(1)} %collective-permute-done.10) | copy-start | bytes 294916
  35.0 7.9 %collective-permute-start.11 = (bf16[8,2,3072]{2,1,0:T(2,128)(2,1)S(1)}, bf16[8,2,3072]{2,1,0:T(2,128)(2,1)S(1)}, u32[]{:S(2)}, u32[]{:S(2)}) collective-permute-start(bf16[8,2,3072]{2,1,0:T(2,128)(2,1)S(1)} %collective-permute-done.10), channel_id=1, source_target_pairs={{0,15},{1,0},{2,1},{3,2},{4,3},{5,4},{6,5},{7,6},{8,7},{9,8},{10,9... | collective-permute-start | bytes 294920 | tf_op jit(solution)/shard_map/ppermute | solution.py:22
  42.9 8.0 %copy-start.20 = (bf16[8,2,3072]{2,1,0:T(2,128)(2,1)}, bf16[8,2,3072]{2,1,0:T(2,128)(2,1)S(1)}, u32[]{:S(2)}) copy-start(bf16[8,2,3072]{2,1,0:T(2,128)(2,1)S(1)} %collective-permute-done.3) | copy-start | bytes 294916
  42.9 7.9 %collective-permute-start.4 = (bf16[8,2,3072]{2,1,0:T(2,128)(2,1)S(1)}, bf16[8,2,3072]{2,1,0:T(2,128)(2,1)S(1)}, u32[]{:S(2)}, u32[]{:S(2)}) collective-permute-start(bf16[8,2,3072]{2,1,0:T(2,128)(2,1)S(1)} %collective-permute-done.3), channel_id=1, source_target_pairs={{0,1},{1,2},{2,3},{3,4},{4,5},{5,6},{6,7},{7,8},{8,9},{9,10},{10,1... | collective-permute-start | bytes 294920 | tf_op jit(solution)/shard_map/ppermute | solution.py:20
  42.9 17.7 %copy-start.21 = (bf16[8,2,3072]{2,1,0:T(2,128)(2,1)}, bf16[8,2,3072]{2,1,0:T(2,128)(2,1)S(1)}, u32[]{:S(2)}) copy-start(bf16[8,2,3072]{2,1,0:T(2,128)(2,1)S(1)} %collective-permute-done.11) | copy-start | bytes 294916
  42.9 17.7 %collective-permute-start.12 = (bf16[8,2,3072]{2,1,0:T(2,128)(2,1)S(1)}, bf16[8,2,3072]{2,1,0:T(2,128)(2,1)}, u32[]{:S(2)}, u32[]{:S(2)}) collective-permute-start(bf16[8,2,3072]{2,1,0:T(2,128)(2,1)S(1)} %collective-permute-done.11), channel_id=1, source_target_pairs={{0,15},{1,0},{2,1},{3,2},{4,3},{5,4},{6,5},{7,6},{8,7},{9,8},{10,9... | collective-permute-start | bytes 294920 | tf_op jit(solution)/shard_map/ppermute | solution.py:22
  50.8 9.8 %copy-start.22 = (bf16[8,2,3072]{2,1,0:T(2,128)(2,1)}, bf16[8,2,3072]{2,1,0:T(2,128)(2,1)S(1)}, u32[]{:S(2)}) copy-start(bf16[8,2,3072]{2,1,0:T(2,128)(2,1)S(1)} %collective-permute-done.4) | copy-start | bytes 294916
  50.8 15.2 %collective-permute-start.5 = (bf16[8,2,3072]{2,1,0:T(2,128)(2,1)S(1)}, bf16[8,2,3072]{2,1,0:T(2,128)(2,1)}, u32[]{:S(2)}, u32[]{:S(2)}) collective-permute-start(bf16[8,2,3072]{2,1,0:T(2,128)(2,1)S(1)} %collective-permute-done.4), channel_id=1, source_target_pairs={{0,1},{1,2},{2,3},{3,4},{4,5},{5,6},{6,7},{7,8},{8,9},{9,10},{10,1... | collective-permute-start | bytes 294920 | tf_op jit(solution)/shard_map/ppermute | solution.py:20
  56.2 10.0 %copy-start.28 = (f32[2,2,128]{2,1,0:T(2,128)S(1)}, f32[2,2,128]{2,1,0:T(2,128)}, u32[]{:S(2)}) copy-start(f32[2,2,128]{2,1,0:T(2,128)} %param.32) | copy-start | bytes 6148
  56.2 26.9 %copy-start.5 = (bf16[8,2,3072]{2,1,0:T(2,128)(2,1)S(1)}, bf16[8,2,3072]{2,1,0:T(2,128)(2,1)}, u32[]{:S(2)}) copy-start(bf16[8,2,3072]{2,1,0:T(2,128)(2,1)} %param.19) | copy-start | bytes 294916
  60.6 9.0 %collective-permute-start.13 = (bf16[8,2,3072]{2,1,0:T(2,128)(2,1)}, bf16[8,2,3072]{2,1,0:T(2,128)(2,1)}, u32[]{:S(2)}, u32[]{:S(2)}) collective-permute-start(bf16[8,2,3072]{2,1,0:T(2,128)(2,1)} %collective-permute-done.12), channel_id=1, source_target_pairs={{0,15},{1,0},{2,1},{3,2},{4,3},{5,4},{6,5},{7,6},{8,7},{9,8},{10,9... | collective-permute-start | bytes 294920 | tf_op jit(solution)/shard_map/ppermute | solution.py:22
  66.0 8.9 %collective-permute-start.6 = (bf16[8,2,3072]{2,1,0:T(2,128)(2,1)}, bf16[8,2,3072]{2,1,0:T(2,128)(2,1)}, u32[]{:S(2)}, u32[]{:S(2)}) collective-permute-start(bf16[8,2,3072]{2,1,0:T(2,128)(2,1)} %collective-permute-done.5), channel_id=1, source_target_pairs={{0,1},{1,2},{2,3},{3,4},{4,5},{5,6},{6,7},{7,8},{8,9},{9,10},{10,1... | collective-permute-start | bytes 294920 | tf_op jit(solution)/shard_map/ppermute | solution.py:20
  69.6 7.9 %collective-permute-start.14 = (bf16[8,2,3072]{2,1,0:T(2,128)(2,1)}, bf16[8,2,3072]{2,1,0:T(2,128)(2,1)S(1)}, u32[]{:S(2)}, u32[]{:S(2)}) collective-permute-start(bf16[8,2,3072]{2,1,0:T(2,128)(2,1)} %collective-permute-done.13), channel_id=1, source_target_pairs={{0,15},{1,0},{2,1},{3,2},{4,3},{5,4},{6,5},{7,6},{8,7},{9,8},{10,9... | collective-permute-start | bytes 294920 | tf_op jit(solution)/shard_map/ppermute | solution.py:22
  74.9 8.1 %collective-permute-start.7 = (bf16[8,2,3072]{2,1,0:T(2,128)(2,1)}, bf16[8,2,3072]{2,1,0:T(2,128)(2,1)S(1)}, u32[]{:S(2)}, u32[]{:S(2)}) collective-permute-start(bf16[8,2,3072]{2,1,0:T(2,128)(2,1)} %collective-permute-done.6), channel_id=1, source_target_pairs={{0,1},{1,2},{2,3},{3,4},{4,5},{5,6},{6,7},{7,8},{8,9},{9,10},{10,1... | collective-permute-start | bytes 294920 | tf_op jit(solution)/shard_map/ppermute | solution.py:20
  83.1 26.4 %copy-start.25 = (f32[8,3072]{1,0:T(8,128)S(1)}, f32[8,3072]{1,0:T(8,128)}, u32[]{:S(2)}) copy-start(f32[8,3072]{1,0:T(8,128)} %get-tuple-element.26) | copy-start | bytes 294916
  83.1 26.4 %copy-start.26 = (f32[8,3072]{1,0:T(8,128)S(1)}, f32[8,3072]{1,0:T(8,128)}, u32[]{:S(2)}) copy-start(f32[8,3072]{1,0:T(8,128)} %get-tuple-element.27) | copy-start | bytes 294916
  113.9 8.6 %copy-start.12 = (f32[8,3072]{1,0:T(8,128)S(1)}, f32[8,3072]{1,0:T(8,128)}, u32[]{:S(2)}) copy-start(f32[8,3072]{1,0:T(8,128)} %get-tuple-element.32) | copy-start | bytes 294916
  113.9 8.6 %copy-start.13 = (f32[8,3072]{1,0:T(8,128)S(1)}, f32[8,3072]{1,0:T(8,128)}, u32[]{:S(2)}) copy-start(f32[8,3072]{1,0:T(8,128)} %get-tuple-element.33) | copy-start | bytes 294916
  134.3 12.0 %copy-start.29 = (f32[128]{0:T(128)S(1)}, f32[128]{0:T(128)}, u32[]{:S(2)}) copy-start(f32[128]{0:T(128)} %get-tuple-element.41) | copy-start | bytes 1540
  134.3 12.0 %copy-start.30 = (f32[128]{0:T(128)S(1)}, f32[128]{0:T(128)}, u32[]{:S(2)}) copy-start(f32[128]{0:T(128)} %get-tuple-element.43) | copy-start | bytes 1540
  143.2 8.5 %copy-start.31 = (s32[8]{0:T(128)S(1)}, s32[8]{0:T(128)}, u32[]{:S(2)}) copy-start(s32[8]{0:T(128)} %param.23) | copy-start | bytes 100
  149.9 81.2 %all-gather.9.cloned.1.call-start = ((), (), s32[]{:S(2)}) async-start(), calls=%async_computation.5 | async-start | bytes 3342336 | tf_op jit(solution)/shard_map/all_gather | solution.py:165
  151.6 172.9 %reduce-scatter.4.cloned.1.call-start = ((), (), s32[]{:S(2)}) async-start(), calls=%async_computation.6 | async-start | bytes 6684672 | tf_op jit(solution)/shard_map/reduce_scatter | solution.py:194
  238.9 85.6 %copy-start.7 = (bf16[8,2,2,3072]{3,2,1,0:T(2,128)(2,1)S(1)}, bf16[8,2,2,3072]{3,2,1,0:T(2,128)(2,1)}, u32[]{:S(2)}) copy-start(bf16[8,2,2,3072]{3,2,1,0:T(2,128)(2,1)} %param.18) | copy-start | bytes 589828
  238.9 85.6 %copy-start.9 = (f32[8,3072]{1,0:T(8,128)S(1)}, f32[8,3072]{1,0:T(8,128)}, u32[]{:S(2)}) copy-start(f32[8,3072]{1,0:T(8,128)} %get-tuple-element.31) | copy-start | bytes 294916
  239.0 140.8 %all-gather.11.cloned.1.call-start = ((), (), s32[]{:S(2)}) async-start(), calls=%async_computation.7 | async-start | bytes 3342336 | tf_op jit(solution)/shard_map/all_gather | solution.py:199
  326.8 161.8 %reduce-scatter.6.cloned.1.call-start = ((), (), s32[]{:S(2)}) async-start(), calls=%async_computation.8 | async-start | bytes 6684672 | tf_op jit(solution)/shard_map/reduce_scatter | solution.py:214
  402.9 169.6 %reduce-scatter.8.cloned.1.call-start = ((), (), s32[]{:S(2)}) async-start(), calls=%async_computation.9 | async-start | bytes 3342336 | tf_op jit(solution)/shard_map/reduce_scatter | solution.py:195
  406.3 82.3 %copy-start.10 = (f32[8,3072]{1,0:T(8,128)S(1)}, f32[8,3072]{1,0:T(8,128)}, u32[]{:S(2)}) copy-start(f32[8,3072]{1,0:T(8,128)} %get-tuple-element.28) | copy-start | bytes 294916
  406.3 85.0 %copy-start.11 = (bf16[3072,64]{0,1:T(8,128)(2,1)S(1)}, bf16[3072,64]{0,1:T(8,128)(2,1)}, u32[]{:S(2)}) copy-start(bf16[3072,64]{0,1:T(8,128)(2,1)} %param.35) | copy-start | bytes 1179652
  406.3 85.3 %copy-start.27 = (f32[8,2,128]{2,1,0:T(2,128)S(1)}, f32[8,2,128]{2,1,0:T(2,128)}, u32[]{:S(2)}) copy-start(f32[8,2,128]{2,1,0:T(2,128)} %param.20) | copy-start | bytes 24580
  491.8 83.3 %collective-permute-start.15 = (f32[8,1,128]{2,1,0:T(1,128)S(1)}, f32[8,1,128]{2,1,0:T(1,128)S(1)}, u32[]{:S(2)}, u32[]{:S(2)}) collective-permute-start(f32[8,1,128]{2,1,0:T(1,128)S(1)} %get-tuple-element.38), channel_id=1, source_target_pairs={{0,16},{16,32},{32,48},{48,64},{64,80},{80,96},{96,112},{112,128},... | collective-permute-start | bytes 12296 | tf_op jit(solution)/shard_map/ppermute | solution.py:34
  493.7 81.4 %collective-permute-start.16 = (f32[8,1,128]{2,1,0:T(1,128)S(1)}, f32[8,1,128]{2,1,0:T(1,128)S(1)}, u32[]{:S(2)}, u32[]{:S(2)}) collective-permute-start(f32[8,1,128]{2,1,0:T(1,128)S(1)} %get-tuple-element.39), channel_id=1, source_target_pairs={{16,0},{32,16},{48,32},{64,48},{80,64},{96,80},{112,96},{128,112},... | collective-permute-start | bytes 12296 | tf_op jit(solution)/shard_map/ppermute | solution.py:35
  (9 other events, 27.4 us)
Sparse Core Ops, SparseCore 0:
  11.0 58.1 all-gather.4
  150.0 38.9 all-gather.6
  191.5 39.6 all-gather.8
  239.1 85.4 reduce-scatter.3
  327.4 52.3 all-gather.10
  403.0 85.5 reduce-scatter.5
  492.2 80.2 reduce-scatter.7
